TPU v7x, 256 devices: a whole 4x4x8 slice. The times are simulated.
256 devices in a mesh: gx: 32 (over z_hi, x, core), gy: 4 (over y), gz: 2 (over z_lo).
Axes of the slice: x: 4, y: 4, z: 8 (z_hi: 4, z_lo: 2; z = z_hi * 2 + z_lo), core: 2. Of those that a mesh axis runs over, the one named last changes fastest.
Arguments:
- unary: bfloat16 [128, 32, 128, 128], P('gx', 'gy', 'gz'), may hold values from -3 to 3
- compat: float32 [6, 128, 128], replicated, may hold values from -2.5 to 2.5
- saved_first: bfloat16 [6, 128, 32, 128, 128], P(None, 'gx', 'gy', 'gz'), may hold values from 0.25 to 4
- saved_second: bfloat16 [6, 128, 32, 128, 128], P(None, 'gx', 'gy', 'gz'), may hold values from 0.25 to 4
- cotangent: float32 [128, 32, 128, 128], P('gx', 'gy', 'gz'), may hold values from -6 to 6
Outputs:
- grad_unary: float32 [128, 32, 128, 128], P('gx', 'gy', 'gz')
- grad_compat: float32 [6, 128, 128], replicated
All inputs are finite; a program needn't handle non-finite values.
Results may differ from a plain program's by a relative error of at most 0.0084.
Values may be sent and summed in bfloat16 or wider, within the bound.
No kernel may reach another device: no remote copies, remote signals or barrier semaphores. Data moves between devices by JAX's collectives and lax.ppermute only.
A program may use at most 128 MiB of HBM per device.

v0:
```python
import jax
import jax.numpy as jnp
from jax import lax
from jax.sharding import PartitionSpec as P

OPPOSE = (1, 0, 3, 2, 5, 4)


def extended(cells, sides, width):
    for axis, dim in sides:
        count = lax.axis_size(axis)
        ends = count - 1
        head = lax.slice_in_dim(cells, 0, width, axis=dim)
        tail = lax.slice_in_dim(cells, cells.shape[dim] - width, cells.shape[dim], axis=dim)
        cells = jnp.concatenate(
            [
                lax.ppermute(tail, axis, [(i, (i + 1) % count) for i in range(ends)]),
                cells,
                lax.ppermute(head, axis, [((i + 1) % count, i) for i in range(ends)]),
            ],
            axis=dim,
        )
    return cells


def full_product(fields):
    result = fields[0]
    for index in range(1, 6):
        result = result * fields[index]
    return result


def send_terms(potential, messages, whole, weights_b):
    labels = potential.shape[-1]
    scaled = potential * whole
    hidden = [scaled / messages[OPPOSE[direction]] for direction in range(6)]
    hidden_b = jnp.stack(hidden).astype(jnp.bfloat16)
    outgoing = jnp.einsum(
        "dxyzk,dkl->dxyzl", hidden_b, weights_b, preferred_element_type=jnp.float32
    )
    totals = jnp.sum(outgoing, axis=-1, keepdims=True)
    normal = labels * outgoing / totals
    return (hidden_b, normal, totals)


def trade(low_face, high_face, axis_dim):
    packed = jnp.concatenate([low_face, high_face], axis=axis_dim)
    if axis_dim == 0:
        rims = extended(packed, (("gx", 0),), 1)
    elif axis_dim == 1:
        rims = extended(packed, (("gy", 1),), 1)
    else:
        rims = extended(packed, (("gz", 2),), 1)
    lower = lax.slice_in_dim(rims, 0, 1, axis=axis_dim)
    upper = lax.slice_in_dim(rims, 3, 4, axis=axis_dim)
    return (lower, upper)


def spread(normal_b, lower_edge, upper_edge):
    result = []
    for axis_dim in range(3):
        plus = normal_b[2 * axis_dim]
        minus = normal_b[2 * axis_dim + 1]
        length = plus.shape[axis_dim]
        lower, upper = trade(
            lax.slice_in_dim(minus, 0, 1, axis=axis_dim),
            lax.slice_in_dim(plus, length - 1, length, axis=axis_dim),
            axis_dim,
        )
        ones = jnp.ones_like(lower)
        lower = jnp.where(lower_edge[axis_dim], ones, lower)
        upper = jnp.where(upper_edge[axis_dim], ones, upper)
        result.append(
            jnp.concatenate(
                [lower, lax.slice_in_dim(plus, 0, length - 1, axis=axis_dim)], axis=axis_dim
            )
        )
        result.append(
            jnp.concatenate(
                [lax.slice_in_dim(minus, 1, length, axis=axis_dim), upper], axis=axis_dim
            )
        )
    return result


def gather_back(grad_b):
    result = []
    for axis_dim in range(3):
        plus = grad_b[2 * axis_dim]
        minus = grad_b[2 * axis_dim + 1]
        length = plus.shape[axis_dim]
        lower, upper = trade(
            lax.slice_in_dim(plus, 0, 1, axis=axis_dim),
            lax.slice_in_dim(minus, length - 1, length, axis=axis_dim),
            axis_dim,
        )
        result.append(
            jnp.concatenate(
                [lax.slice_in_dim(plus, 1, length, axis=axis_dim), upper], axis=axis_dim
            )
        )
        result.append(
            jnp.concatenate(
                [lower, lax.slice_in_dim(minus, 0, length - 1, axis=axis_dim)], axis=axis_dim
            )
        )
    return jnp.stack(result).astype(jnp.float32)


def belief_adjoint(potential, arriving, cotangent):
    labels = potential.shape[-1]
    whole = full_product(arriving)
    joint = potential * whole
    summed = jnp.sum(joint, axis=-1, keepdims=True)
    belief = joint / summed
    grad_joint = labels * (cotangent - jnp.sum(cotangent * belief, axis=-1, keepdims=True)) / summed
    grad_potential = grad_joint * whole
    scaled = grad_joint * joint
    grad_arriving = [(scaled / arriving[edge]).astype(jnp.bfloat16) for edge in range(6)]
    return (grad_arriving, grad_potential)


def local_adjoint(grad_normal, normal, totals, hidden_b, weights_b):
    labels = normal.shape[-1]
    inner = jnp.sum(grad_normal * normal, axis=-1, keepdims=True)
    grad_out = (labels / totals * (grad_normal - inner / labels)).astype(jnp.bfloat16)
    grad_weights = jnp.einsum(
        "dxyzk,dxyzl->dkl", hidden_b, grad_out, preferred_element_type=jnp.float32
    )
    grad_hidden = jnp.einsum(
        "dxyzl,dkl->dxyzk", grad_out, weights_b, preferred_element_type=jnp.float32
    )
    return (grad_weights, grad_hidden)


def adjoint_terms(grad_hidden, potential, messages, whole):
    ratios = [grad_hidden[OPPOSE[index]] / messages[index] for index in range(6)]
    total = ratios[0]
    for index in range(1, 6):
        total = total + ratios[index]
    unary_term = whole * total
    scaled = potential * whole
    grad_messages = []
    for edge in range(6):
        partial_sum = None
        for index in range(6):
            if index == edge:
                continue
            partial_sum = ratios[index] if partial_sum is None else partial_sum + ratios[index]
        grad_messages.append((partial_sum * (scaled / messages[edge])).astype(jnp.bfloat16))
    return (unary_term, grad_messages)


def body(unary, compat, saved_first, saved_second, cotangent):
    potential = jnp.exp(unary.astype(jnp.float32))
    weights = jnp.exp(compat)
    weights_b = weights.astype(jnp.bfloat16)
    lower_edge = (lax.axis_index("gx") == 0, lax.axis_index("gy") == 0, lax.axis_index("gz") == 0)
    upper_edge = (
        lax.axis_index("gx") == lax.axis_size("gx") - 1,
        lax.axis_index("gy") == lax.axis_size("gy") - 1,
        lax.axis_index("gz") == lax.axis_size("gz") - 1,
    )
    first = [saved_first[index].astype(jnp.float32) for index in range(6)]
    second = [saved_second[index].astype(jnp.float32) for index in range(6)]
    whole_two = full_product(second)
    hidden_two, normal_two, totals_two = send_terms(potential, second, whole_two, weights_b)
    arriving = spread(
        [normal_two[index].astype(jnp.bfloat16) for index in range(6)], lower_edge, upper_edge
    )
    arriving = [value.astype(jnp.float32) for value in arriving]
    grad_arriving, grad_potential = belief_adjoint(potential, arriving, cotangent)
    grad_normal_two = gather_back(grad_arriving)
    weights_two, grad_hidden_two = local_adjoint(
        grad_normal_two, normal_two, totals_two, hidden_two, weights_b
    )
    unary_two, grad_second = adjoint_terms(grad_hidden_two, potential, second, whole_two)
    grad_potential = grad_potential + unary_two
    whole_one = full_product(first)
    hidden_one, normal_one, totals_one = send_terms(potential, first, whole_one, weights_b)
    grad_normal_one = gather_back(grad_second)
    weights_one, grad_hidden_one = local_adjoint(
        grad_normal_one, normal_one, totals_one, hidden_one, weights_b
    )
    ratios_one = [grad_hidden_one[OPPOSE[index]] / first[index] for index in range(6)]
    total_one = ratios_one[0]
    for index in range(1, 6):
        total_one = total_one + ratios_one[index]
    grad_potential = grad_potential + whole_one * total_one
    grad_unary = potential * grad_potential
    summed = lax.psum(weights_two + weights_one, ("gx", "gy", "gz"))
    grad_compat = weights * summed
    return (grad_unary, grad_compat)


def solution(mesh):
    placed = (
        P("gx", "gy", "gz", None),
        P(),
        P(None, "gx", "gy", "gz", None),
        P(None, "gx", "gy", "gz", None),
        P("gx", "gy", "gz", None),
    )
    return jax.shard_map(
        body,
        mesh=mesh,
        in_specs=placed,
        out_specs=(P("gx", "gy", "gz", None), P()),
        check_vma=False,
    )
```

profile of v0, /device:TPU:1, one launch (start us, length us, event | category | flops | bytes accessed | tf_op | source)
XLA Modules:
  0.0 413.3 jit_solution(10263491536333653765)
XLA Ops:
  7.2 4.7 %bitcast_dynamic-update-slice_fusion.5 = (bf16[6,4,8,64,128]{4,3,2,1,0:T(8,128)(2,1)S(1)}, f32[4,8,64,128]{3,2,1,0:T(8,128)S(1)}, bf16[6,4,8,64,128]{4,3,2,1,0:T(8,128)(2,1)S(1)}, f32[4,8,64,128]{3,2,1,0:T(8,128)S(1)}) fusion(bf16[6,4,8,64,128]{4,3,2,1,0:T(8,128)(2,1)} %param.7, bf16[4,8,64,128]{3,2,1,0:T(8,128)(2,1)} %param.5, ...), kind=kLoop, calls=%fused_computation.152 | loop fusion | flops 7602174 | bytes 9961472
  15.0 1.9 fusion.77
  17.0 2.0 fusion.13
  20.5 1.3 collective-permute-start.3
  22.4 5.3 %collective-permute-start.2 = (bf16[4,1,64,128]{3,2,1,0:T(8,128)(2,1)}, bf16[4,1,64,128]{3,2,1,0:T(8,128)(2,1)}, u32[]{:S(2)}, u32[]{:S(2)}) collective-permute-start(bf16[4,1,64,128]{3,2,1,0:T(8,128)(2,1)} %slice.289), channel_id=1, source_target_pairs={{0,2},{2,4},{4,6},{1,3},{3,5},{5,7},{8,10},{10,12},{12,14},{9,11},... | collective-permute-start | bytes 196616 | tf_op jit(solution)/shard_map/ppermute | solution.py:17
  30.1 4.6 %collective-permute-start.4 = (bf16[4,8,1,128]{3,2,1,0:T(2,128)(2,1)}, bf16[4,8,1,128]{3,2,1,0:T(2,128)(2,1)S(1)}, u32[]{:S(2)}, u32[]{:S(2)}) collective-permute-start(bf16[4,8,1,128]{3,2,1,0:T(2,128)(2,1)} %slice.295), channel_id=1, source_target_pairs={{0,1},{2,3},{4,5},{6,7},{8,9},{10,11},{12,13},{14,15},{16,17},{18,... | collective-permute-start | bytes 24584 | tf_op jit(solution)/shard_map/ppermute | solution.py:17
  35.4 5.6 %collective-permute-start.1 = (bf16[1,8,64,128]{3,2,1,0:T(8,128)(2,1)}, bf16[1,8,64,128]{3,2,1,0:T(8,128)(2,1)}, u32[]{:S(2)}, u32[]{:S(2)}) collective-permute-start(bf16[1,8,64,128]{3,2,1,0:T(8,128)(2,1)} %get-tuple-element.20), channel_id=1, source_target_pairs={{8,0},{16,8},{24,16},{32,24},{40,32},{48,40},{56,48},{64,56},{72,6... | collective-permute-start | bytes 393224 | tf_op jit(solution)/shard_map/ppermute | solution.py:19
  42.4 4.4 %fusion.78 = (f32[6,4,8,64]{3,2,1,0:T(8,128)S(1)}, f32[6,4,8,64,128]{4,3,2,1,0:T(8,128)}) fusion(bf16[6,4,8,64,128]{4,3,2,1,0:T(8,128)(2,1)S(1)} %bitcast_dynamic-update-slice_fusion, bf16[6,128,128,1,1]{2,1,4,3,0:T(8,128)(2,1)S(1)} %fusion.68), kind=kOutput, calls=%fused_computation.182 | convolution fusion | flops 404213760 | bytes 9682944 | tf_op jit(solution)/shard_map/dxyzk,dkl->dxyzl/dot_general | solution.py:38
  49.5 2.2 collective-permute-start
  54.4 2.0 fusion.72
  56.5 11.9 %fusion.37 = (bf16[4,8,64,128]{3,2,1,0:T(8,128)(2,1)S(1)}, f32[4,8,64,128]{3,2,1,0:T(8,128)S(1)}, f32[4,8,64,128]{3,2,1,0:T(8,128)}) fusion(bf16[4,8,1,128]{3,2,1,0:T(2,128)(2,1)S(1)} %broadcast_select_fusion.4, bf16[4,8,63,128]{3,2,1,0:T(8,128)(2,1)S(1)} %copy-done.14, f32[4,8,64,128]{3,2,1,0:T(8,128)S(1)} %get-tuple-element.13, ...), kind=kOutput, calls=%fused_computation.75 | output fusion | flops 4196479 | bytes 5775360 | tf_op jit(solution)/shard_map/sub | solution.py:116
  69.3 2.5 collective-permute-start.6
  71.8 3.2 collective-permute-start.7
  75.4 1.4 collective-permute-start.8
  76.8 4.0 collective-permute-start.9
  80.8 1.3 collective-permute-start.10
  82.2 4.0 collective-permute-start.11
  87.3 3.8 fusion.1
  91.1 5.5 %fusion.79 = f32[6,4,8,64,128]{4,3,2,1,0:T(8,128)S(1)} fusion(bf16[6,128,128,1,1]{2,1,4,3,0:T(8,128)(2,1)S(1)} %fusion.68, bf16[6,4,8,64,128]{4,3,2,1,0:T(8,128)(2,1)S(1)} %fusion.60, f32[6,4,8,64]{3,2,1,0:T(8,128)S(1)} %broadcast_multiply_fusion.1, f32[6,4,8,64]{3,2,1,0:T(8,128)S(1)} %copy-done.18), kind=kOutput, calls=%fused_computation.183 | convolution fusion | flops 408944640 | bytes 9732096 | tf_op jit(solution)/shard_map/dxyzl,dkl->dxyzk/dot_general | solution.py:130
  100.4 4.2 %collective-permute-start.13 = (bf16[1,8,64,128]{3,2,1,0:T(8,128)(2,1)S(1)}, bf16[1,8,64,128]{3,2,1,0:T(8,128)(2,1)S(1)}, u32[]{:S(2)}, u32[]{:S(2)}) collective-permute-start(bf16[1,8,64,128]{3,2,1,0:T(8,128)(2,1)S(1)} %slice.320), channel_id=1, source_target_pairs={{0,8},{8,16},{16,24},{24,32},{32,40},{40,48},{48,56},{56,64},{64,7... | collective-permute-start | bytes 393224 | tf_op jit(solution)/shard_map/ppermute | solution.py:17
  104.7 2.2 collective-permute-start.12
  106.9 5.7 %fusion.17 = f32[6,128,128]{2,1,0:T(8,128)S(1)} fusion(bf16[6,4,8,64,128]{4,3,2,1,0:T(8,128)(2,1)S(1)} %copy-done.10, bf16[6,4,8,64,128]{4,3,2,1,0:T(8,128)(2,1)S(1)} %fusion.60, f32[6,4,8,64]{3,2,1,0:T(8,128)S(1)} %broadcast_multiply_fusion.1, f32[6,4,8,64]{3,2,1,0:T(8,128)S(1)} %copy-done.18), kind=kOutput, calls=%fused_computation.67 | convolution fusion | flops 408944640 | bytes 6782976 | tf_op jit(solution)/shard_map/dxyzk,dxyzl->dkl/dot_general | solution.py:127
  112.9 1.3 collective-permute-start.14
  114.2 4.0 collective-permute-start.15
  118.2 1.3 collective-permute-start.16
  119.5 4.2 %collective-permute-start.17 = (bf16[4,8,1,128]{3,2,1,0:T(2,128)(2,1)S(1)}, bf16[4,8,1,128]{3,2,1,0:T(2,128)(2,1)S(1)}, u32[]{:S(2)}, u32[]{:S(2)}) collective-permute-start(bf16[4,8,1,128]{3,2,1,0:T(2,128)(2,1)S(1)} %slice.328), channel_id=1, source_target_pairs={{0,1},{2,3},{4,5},{6,7},{8,9},{10,11},{12,13},{14,15},{16,17},{18,... | collective-permute-start | bytes 24584 | tf_op jit(solution)/shard_map/ppermute | solution.py:17
  124.6 3.8 fusion.4
  128.5 6.8 %fusion.80 = f32[6,4,8,64,128]{4,3,2,1,0:T(8,128)} fusion(bf16[6,128,128,1,1]{2,1,4,3,0:T(8,128)(2,1)S(1)} %fusion.68, bf16[6,4,8,64,128]{4,3,2,1,0:T(8,128)(2,1)S(1)} %fusion.66, f32[6,4,8,64]{3,2,1,0:T(8,128)S(1)} %broadcast_multiply_fusion, f32[6,4,8,64]{3,2,1,0:T(8,128)S(1)} %broadcast_divide_fusion), kind=kOutput, calls=%fused_computation.184 | convolution fusion | flops 408944640 | bytes 9732096 | tf_op jit(solution)/shard_map/dxyzl,dkl->dxyzk/dot_general | solution.py:130
  135.3 6.2 %fusion.27 = f32[6,128,128]{2,1,0:T(8,128)} fusion(f32[6,128,128]{2,1,0:T(8,128)S(1)} %fusion.17, bf16[6,4,8,64,128]{4,3,2,1,0:T(8,128)(2,1)S(1)} %copy-done.8, bf16[6,4,8,64,128]{4,3,2,1,0:T(8,128)(2,1)S(1)} %fusion.66, f32[6,4,8,64]{3,2,1,0:T(8,128)S(1)} %broadcast_multiply_fusion, f32[6,4,8,64]{3,2,1,0:T(8,128)S(1)} %broadcast_divide_fusion), kind=kOutput, calls=%fused_computation.69 | convolution fusion | flops 409042944 | bytes 7176192 | tf_op jit(solution)/shard_map/dxyzk,dxyzl->dkl/dot_general | solution.py:127
  141.5 7.3 %fusion.46 = f32[4,8,64,128]{3,2,1,0:T(8,128)} fusion(f32[6,4,8,64,128]{4,3,2,1,0:T(8,128)} %fusion.80, f32[4,8,64,128]{3,2,1,0:T(8,128)S(1)} %get-tuple-element.9, f32[4,8,64,128]{3,2,1,0:T(8,128)} %get-tuple-element.36, f32[4,8,64,128]{3,2,1,0:T(8,128)} %copy-done.11, bf16[4,8,64,128]{3,2,1,0:T(8,128)(2,1)} %param.5, f32[4,8,64,128]{3,2,1,0:T(8,128)S(1)} %copy-done.5, ...), kind=kLoop, calls=%fused_computation.84 | loop fusion | flops 11010048 | bytes 19398656 | tf_op jit(solution)/shard_map/mul | solution.py:190
  148.9 255.7 %all-reduce.2.cloned.1.call-done = f32[6,128,128]{2,1,0:T(8,128)} async-done(((f32[6,128,128]{2,1,0:T(8,128)}), f32[6,128,128]{2,1,0:T(8,128)}) %all-reduce.2.cloned.1.call-update) | async-done | bytes 393232 | tf_op jit(solution)/shard_map/psum | solution.py:191
  404.5 1.9 exponential_multiply_fusion
  (141 shorter events, 22.2 us)
Async XLA Ops:
  7.2 397.4 %all-reduce.2.cloned.1.call-start = ((), (), s32[]{:S(2)}) async-start(), calls=%async_computation | async-start | bytes 786432 | tf_op jit(solution)/shard_map/psum | solution.py:191
  19.8 22.6 %copy-start.16 = (bf16[4,8,64,128]{3,2,1,0:T(8,128)(2,1)}, bf16[4,8,64,128]{3,2,1,0:T(8,128)(2,1)S(1)}, u32[]{:S(2)}) copy-start(bf16[4,8,64,128]{3,2,1,0:T(8,128)(2,1)S(1)} %get-tuple-element.26) | copy-start | bytes 1572868
  20.5 32.1 %collective-permute-start.3 = (bf16[4,1,64,128]{3,2,1,0:T(8,128)(2,1)}, bf16[4,1,64,128]{3,2,1,0:T(8,128)(2,1)}, u32[]{:S(2)}, u32[]{:S(2)}) collective-permute-start(bf16[4,1,64,128]{3,2,1,0:T(8,128)(2,1)} %slice.293), channel_id=1, source_target_pairs={{2,0},{4,2},{6,4},{3,1},{5,3},{7,5},{10,8},{12,10},{14,12},{11,9},... | collective-permute-start | bytes 196616 | tf_op jit(solution)/shard_map/ppermute | solution.py:19
  22.4 31.1 %collective-permute-start.2 = (bf16[4,1,64,128]{3,2,1,0:T(8,128)(2,1)}, bf16[4,1,64,128]{3,2,1,0:T(8,128)(2,1)}, u32[]{:S(2)}, u32[]{:S(2)}) collective-permute-start(bf16[4,1,64,128]{3,2,1,0:T(8,128)(2,1)} %slice.289), channel_id=1, source_target_pairs={{0,2},{2,4},{4,6},{1,3},{3,5},{5,7},{8,10},{10,12},{12,14},{9,11},... | collective-permute-start | bytes 196616 | tf_op jit(solution)/shard_map/ppermute | solution.py:17
  28.2 21.3 %collective-permute-start.5 = (bf16[4,8,1,128]{3,2,1,0:T(2,128)(2,1)}, bf16[4,8,1,128]{3,2,1,0:T(2,128)(2,1)}, u32[]{:S(2)}, u32[]{:S(2)}) collective-permute-start(bf16[4,8,1,128]{3,2,1,0:T(2,128)(2,1)} %slice.299), channel_id=1, source_target_pairs={{1,0},{3,2},{5,4},{7,6},{9,8},{11,10},{13,12},{15,14},{17,16},{19,... | collective-permute-start | bytes 24584 | tf_op jit(solution)/shard_map/ppermute | solution.py:19
  30.1 22.4 %collective-permute-start.4 = (bf16[4,8,1,128]{3,2,1,0:T(2,128)(2,1)}, bf16[4,8,1,128]{3,2,1,0:T(2,128)(2,1)S(1)}, u32[]{:S(2)}, u32[]{:S(2)}) collective-permute-start(bf16[4,8,1,128]{3,2,1,0:T(2,128)(2,1)} %slice.295), channel_id=1, source_target_pairs={{0,1},{2,3},{4,5},{6,7},{8,9},{10,11},{12,13},{14,15},{16,17},{18,... | collective-permute-start | bytes 24584 | tf_op jit(solution)/shard_map/ppermute | solution.py:17
  35.4 18.0 %collective-permute-start.1 = (bf16[1,8,64,128]{3,2,1,0:T(8,128)(2,1)}, bf16[1,8,64,128]{3,2,1,0:T(8,128)(2,1)}, u32[]{:S(2)}, u32[]{:S(2)}) collective-permute-start(bf16[1,8,64,128]{3,2,1,0:T(8,128)(2,1)} %get-tuple-element.20), channel_id=1, source_target_pairs={{8,0},{16,8},{24,16},{32,24},{40,32},{48,40},{56,48},{64,56},{72,6... | collective-permute-start | bytes 393224 | tf_op jit(solution)/shard_map/ppermute | solution.py:19
  46.8 7.7 %copy-start.6 = (bf16[4,8,64,128]{3,2,1,0:T(8,128)(2,1)S(1)}, bf16[4,8,64,128]{3,2,1,0:T(8,128)(2,1)}, u32[]{:S(2)}) copy-start(bf16[4,8,64,128]{3,2,1,0:T(8,128)(2,1)} %param.5) | copy-start | bytes 1572868
  49.5 7.0 %copy-start.14 = (bf16[4,8,63,128]{3,2,1,0:T(8,128)(2,1)S(1)}, bf16[4,8,63,128]{3,2,1,0:T(8,128)(2,1)}, u32[]{:S(2)}) copy-start(bf16[4,8,63,128]{3,2,1,0:T(8,128)(2,1)} %slice.298) | copy-start | bytes 1548292
  49.5 4.9 %collective-permute-start = (bf16[1,8,64,128]{3,2,1,0:T(8,128)(2,1)}, bf16[1,8,64,128]{3,2,1,0:T(8,128)(2,1)S(1)}, u32[]{:S(2)}, u32[]{:S(2)}) collective-permute-start(bf16[1,8,64,128]{3,2,1,0:T(8,128)(2,1)} %get-tuple-element.19), channel_id=1, source_target_pairs={{0,8},{8,16},{16,24},{24,32},{32,40},{40,48},{48,56},{56,64},{64,7... | collective-permute-start | bytes 393224 | tf_op jit(solution)/shard_map/ppermute | solution.py:17
  56.5 11.9 %copy-start.11 = (f32[4,8,64,128]{3,2,1,0:T(8,128)}, f32[4,8,64,128]{3,2,1,0:T(8,128)S(1)}, u32[]{:S(2)}) copy-start(f32[4,8,64,128]{3,2,1,0:T(8,128)S(1)} %get-tuple-element.13) | copy-start | bytes 3145732
  56.5 11.9 %copy-start.12 = (bf16[3,8,64,128]{3,2,1,0:T(8,128)(2,1)S(1)}, bf16[3,8,64,128]{3,2,1,0:T(8,128)(2,1)}, u32[]{:S(2)}) copy-start(bf16[3,8,64,128]{3,2,1,0:T(8,128)(2,1)} %get-tuple-element.21) | copy-start | bytes 1179652
  56.5 11.9 %copy-start.13 = (bf16[3,8,64,128]{3,2,1,0:T(8,128)(2,1)S(1)}, bf16[3,8,64,128]{3,2,1,0:T(8,128)(2,1)}, u32[]{:S(2)}) copy-start(bf16[3,8,64,128]{3,2,1,0:T(8,128)(2,1)} %get-tuple-element.22) | copy-start | bytes 1179652
  68.4 18.9 %slice-start = ((s8[6291456]{0:T(1024)(128)(4,1)}), s8[4194304]{0:T(1024)(128)(4,1)S(1)}, s32[]{:S(2)}) async-start(s8[6291456]{0:T(1024)(128)(4,1)} %bitcast.353), calls=%async_computation.1 | async-start | bytes 8388608
  69.3 12.9 %collective-permute-start.6 = (bf16[1,8,64,128]{3,2,1,0:T(8,128)(2,1)S(1)}, bf16[1,8,64,128]{3,2,1,0:T(8,128)(2,1)S(1)}, u32[]{:S(2)}, u32[]{:S(2)}) collective-permute-start(bf16[1,8,64,128]{3,2,1,0:T(8,128)(2,1)S(1)} %slice.301), channel_id=1, source_target_pairs={{8,0},{16,8},{24,16},{32,24},{40,32},{48,40},{56,48},{64,56},{72,6... | collective-permute-start | bytes 393224 | tf_op jit(solution)/shard_map/ppermute | solution.py:19
  71.8 14.4 %collective-permute-start.7 = (bf16[1,8,64,128]{3,2,1,0:T(8,128)(2,1)S(1)}, bf16[1,8,64,128]{3,2,1,0:T(8,128)(2,1)S(1)}, u32[]{:S(2)}, u32[]{:S(2)}) collective-permute-start(bf16[1,8,64,128]{3,2,1,0:T(8,128)(2,1)S(1)} %slice.302), channel_id=1, source_target_pairs={{0,8},{8,16},{16,24},{24,32},{32,40},{40,48},{48,56},{56,64},{64,7... | collective-permute-start | bytes 393224 | tf_op jit(solution)/shard_map/ppermute | solution.py:17
  75.1 12.2 %slice-start.1 = ((s8[6291456]{0:T(1024)(128)(4,1)}), s8[2097152]{0:T(1024)(128)(4,1)S(1)}, s32[]{:S(2)}) async-start(s8[6291456]{0:T(1024)(128)(4,1)} %bitcast.353), calls=%async_computation.2 | async-start | bytes 4194304
  75.4 10.9 %collective-permute-start.8 = (bf16[4,1,64,128]{3,2,1,0:T(8,128)(2,1)S(1)}, bf16[4,1,64,128]{3,2,1,0:T(8,128)(2,1)S(1)}, u32[]{:S(2)}, u32[]{:S(2)}) collective-permute-start(bf16[4,1,64,128]{3,2,1,0:T(8,128)(2,1)S(1)} %slice.305), channel_id=1, source_target_pairs={{2,0},{4,2},{6,4},{3,1},{5,3},{7,5},{10,8},{12,10},{14,12},{11,9},... | collective-permute-start | bytes 196616 | tf_op jit(solution)/shard_map/ppermute | solution.py:19
  76.8 9.6 %collective-permute-start.9 = (bf16[4,1,64,128]{3,2,1,0:T(8,128)(2,1)S(1)}, bf16[4,1,64,128]{3,2,1,0:T(8,128)(2,1)S(1)}, u32[]{:S(2)}, u32[]{:S(2)}) collective-permute-start(bf16[4,1,64,128]{3,2,1,0:T(8,128)(2,1)S(1)} %slice.306), channel_id=1, source_target_pairs={{0,2},{2,4},{4,6},{1,3},{3,5},{5,7},{8,10},{10,12},{12,14},{9,11},... | collective-permute-start | bytes 196616 | tf_op jit(solution)/shard_map/ppermute | solution.py:17
  80.8 5.6 %collective-permute-start.10 = (bf16[4,8,1,128]{3,2,1,0:T(2,128)(2,1)S(1)}, bf16[4,8,1,128]{3,2,1,0:T(2,128)(2,1)S(1)}, u32[]{:S(2)}, u32[]{:S(2)}) collective-permute-start(bf16[4,8,1,128]{3,2,1,0:T(2,128)(2,1)S(1)} %slice.309), channel_id=1, source_target_pairs={{1,0},{3,2},{5,4},{7,6},{9,8},{11,10},{13,12},{15,14},{17,16},{19,... | collective-permute-start | bytes 24584 | tf_op jit(solution)/shard_map/ppermute | solution.py:19
  82.2 4.8 %collective-permute-start.11 = (bf16[4,8,1,128]{3,2,1,0:T(2,128)(2,1)S(1)}, bf16[4,8,1,128]{3,2,1,0:T(2,128)(2,1)S(1)}, u32[]{:S(2)}, u32[]{:S(2)}) collective-permute-start(bf16[4,8,1,128]{3,2,1,0:T(2,128)(2,1)S(1)} %slice.310), channel_id=1, source_target_pairs={{0,1},{2,3},{4,5},{6,7},{8,9},{10,11},{12,13},{14,15},{16,17},{18,... | collective-permute-start | bytes 24584 | tf_op jit(solution)/shard_map/ppermute | solution.py:17
  99.2 13.4 %copy-start.15 = (bf16[4,8,64,128]{3,2,1,0:T(8,128)(2,1)}, bf16[4,8,64,128]{3,2,1,0:T(8,128)(2,1)S(1)}, u32[]{:S(2)}) copy-start(bf16[4,8,64,128]{3,2,1,0:T(8,128)(2,1)S(1)} %multiply_convert_fusion.5) | copy-start | bytes 1572868
  99.2 7.7 %copy-start.10 = (bf16[6,4,8,64,128]{4,3,2,1,0:T(8,128)(2,1)S(1)}, bf16[6,4,8,64,128]{4,3,2,1,0:T(8,128)(2,1)}, u32[]{:S(2)}) copy-start(bf16[6,4,8,64,128]{4,3,2,1,0:T(8,128)(2,1)} %copy-done.9) | copy-start | bytes 9437188
  99.2 25.4 %slice-start.2 = ((s8[6291456]{0:T(1024)(128)(4,1)}), s8[2097152]{0:T(1024)(128)(4,1)S(1)}, s32[]{:S(2)}) async-start(s8[6291456]{0:T(1024)(128)(4,1)} %bitcast.355), calls=%async_computation.3 | async-start | bytes 4194304
  100.4 23.4 %collective-permute-start.13 = (bf16[1,8,64,128]{3,2,1,0:T(8,128)(2,1)S(1)}, bf16[1,8,64,128]{3,2,1,0:T(8,128)(2,1)S(1)}, u32[]{:S(2)}, u32[]{:S(2)}) collective-permute-start(bf16[1,8,64,128]{3,2,1,0:T(8,128)(2,1)S(1)} %slice.320), channel_id=1, source_target_pairs={{0,8},{8,16},{16,24},{24,32},{32,40},{40,48},{48,56},{56,64},{64,7... | collective-permute-start | bytes 393224 | tf_op jit(solution)/shard_map/ppermute | solution.py:17
  104.7 20.0 %slice-start.3 = ((s8[6291456]{0:T(1024)(128)(4,1)}), s8[4194304]{0:T(1024)(128)(4,1)S(1)}, s32[]{:S(2)}) async-start(s8[6291456]{0:T(1024)(128)(4,1)} %bitcast.355), calls=%async_computation.4 | async-start | bytes 8388608
  104.7 14.9 %collective-permute-start.12 = (bf16[1,8,64,128]{3,2,1,0:T(8,128)(2,1)S(1)}, bf16[1,8,64,128]{3,2,1,0:T(8,128)(2,1)S(1)}, u32[]{:S(2)}, u32[]{:S(2)}) collective-permute-start(bf16[1,8,64,128]{3,2,1,0:T(8,128)(2,1)S(1)} %slice.319), channel_id=1, source_target_pairs={{8,0},{16,8},{24,16},{32,24},{40,32},{48,40},{56,48},{64,56},{72,6... | collective-permute-start | bytes 393224 | tf_op jit(solution)/shard_map/ppermute | solution.py:19
  112.6 11.2 %slice-start.4 = ((bf16[4,8,64,128]{3,2,1,0:T(8,128)(2,1)}), bf16[3,8,64,128]{3,2,1,0:T(8,128)(2,1)S(1)}, s32[]{:S(2)}) async-start(bf16[4,8,64,128]{3,2,1,0:T(8,128)(2,1)} %copy-done.15), calls=%async_computation.5 | async-start | bytes 786432 | tf_op jit(solution)/shard_map/slice | solution.py:99
  112.9 11.0 %collective-permute-start.14 = (bf16[4,1,64,128]{3,2,1,0:T(8,128)(2,1)S(1)}, bf16[4,1,64,128]{3,2,1,0:T(8,128)(2,1)S(1)}, u32[]{:S(2)}, u32[]{:S(2)}) collective-permute-start(bf16[4,1,64,128]{3,2,1,0:T(8,128)(2,1)S(1)} %slice.323), channel_id=1, source_target_pairs={{2,0},{4,2},{6,4},{3,1},{5,3},{7,5},{10,8},{12,10},{14,12},{11,9},... | collective-permute-start | bytes 196616 | tf_op jit(solution)/shard_map/ppermute | solution.py:19
  114.2 9.8 %collective-permute-start.15 = (bf16[4,1,64,128]{3,2,1,0:T(8,128)(2,1)S(1)}, bf16[4,1,64,128]{3,2,1,0:T(8,128)(2,1)S(1)}, u32[]{:S(2)}, u32[]{:S(2)}) collective-permute-start(bf16[4,1,64,128]{3,2,1,0:T(8,128)(2,1)S(1)} %slice.324), channel_id=1, source_target_pairs={{0,2},{2,4},{4,6},{1,3},{3,5},{5,7},{8,10},{10,12},{12,14},{9,11},... | collective-permute-start | bytes 196616 | tf_op jit(solution)/shard_map/ppermute | solution.py:17
  118.2 5.9 %collective-permute-start.16 = (bf16[4,8,1,128]{3,2,1,0:T(2,128)(2,1)S(1)}, bf16[4,8,1,128]{3,2,1,0:T(2,128)(2,1)S(1)}, u32[]{:S(2)}, u32[]{:S(2)}) collective-permute-start(bf16[4,8,1,128]{3,2,1,0:T(2,128)(2,1)S(1)} %slice.327), channel_id=1, source_target_pairs={{1,0},{3,2},{5,4},{7,6},{9,8},{11,10},{13,12},{15,14},{17,16},{19,... | collective-permute-start | bytes 24584 | tf_op jit(solution)/shard_map/ppermute | solution.py:19
  119.5 4.8 %collective-permute-start.17 = (bf16[4,8,1,128]{3,2,1,0:T(2,128)(2,1)S(1)}, bf16[4,8,1,128]{3,2,1,0:T(2,128)(2,1)S(1)}, u32[]{:S(2)}, u32[]{:S(2)}) collective-permute-start(bf16[4,8,1,128]{3,2,1,0:T(2,128)(2,1)S(1)} %slice.328), channel_id=1, source_target_pairs={{0,1},{2,3},{4,5},{6,7},{8,9},{10,11},{12,13},{14,15},{16,17},{18,... | collective-permute-start | bytes 24584 | tf_op jit(solution)/shard_map/ppermute | solution.py:17
  (12 other events, 48.3 us)
Sparse Core Ops, SparseCore 0:
  141.7 262.8 all-reduce.1
where the time goes:
time: 414 us; the launch traced here: 413 us
  waiting for transfers between devices  256 us (62%)
  starting transfers between devices  53.8 us (13%)
  other arithmetic  48.6 us (12%)
  matrix products  30.4 us (7%)
  between operations  15.1 us (4%)
  local copies, waits for them, and re-layouts  9.02 us (2%)
    psum x1, waiting for transfers between devices, body(): summed = lax.psum(weights_two + weights_one, ('gx', 'gy', 'gz'))  256 us
    ppermute x9, starting transfers between devices, extended(): lax.ppermute(tail, axis, [(i, (i + 1) % count) for i in range(ends)])  35.6 us
    ppermute x9, starting transfers between devices, extended(): lax.ppermute(head, axis, [((i + 1) % count, i) for i in range(ends)])  18.1 us
    dot_general x2, matrix products, local_adjoint(): jnp.einsum('dxyzl,dkl->dxyzk', grad_out, weights_b, preferred_element_typ...  12.3 us
    dot_general x2, matrix products, local_adjoint(): jnp.einsum('dxyzk,dxyzl->dkl', hidden_b, grad_out, preferred_element_type...  11.9 us
    sub x1, other arithmetic, belief_adjoint(): cotangent - jnp.sum(cotangent * belief, axis=-1, keepdims=True)  11.9 us
  transfers between devices with their start and end apart: 19, of which 3 were waited for; matrix products, arithmetic and copies ran while one was open for 7% of the time, Pallas kernels for 0%

commit v1 on v0

--- a/solution.py
+++ b/solution.py
@@ -188,7 +188,7 @@
         total_one = total_one + ratios_one[index]
     grad_potential = grad_potential + whole_one * total_one
     grad_unary = potential * grad_potential
-    summed = lax.psum(weights_two + weights_one, ("gx", "gy", "gz"))
+    summed = jnp.sum(lax.all_gather(weights_two + weights_one, ("gx", "gy", "gz")), axis=0)
     grad_compat = weights * summed
     return (grad_unary, grad_compat)
 

time: 414 us -> 1020 us (2.46)
  waiting for transfers between devices: 256 us -> 830 us
  other arithmetic: 48.6 us -> 75.9 us
    all_gather x0 -> x1, waiting for transfers between devices: none -> 830 us  [body(): lax.all_gather(weights_two + weights_one, ('gx', 'gy', 'gz'))]
    psum x1 -> x0, waiting for transfers between devices: 256 us -> none  [body(): summed = lax.psum(weights_two + weights_one, ('gx', 'gy', 'gz'))]
    reduce_sum x0 -> x1, other arithmetic: none -> 30.8 us  [body(): jnp.sum(lax.all_gather(weights_two + weights_one, ('gx', 'gy', 'gz')), ax...]
  transfers between devices with their start and end apart: 19 -> 19, of which waited for: 3 -> 3; matrix products, arithmetic and copies ran while one was open for 7% -> 3% of each run, Pallas kernels for 0% -> 0%
where the time goes in v1:
time: 1020 us
  waiting for transfers between devices  830 us (81%)
  other arithmetic  75.9 us (7%)
  starting transfers between devices  53 us (5%)
  matrix products  31.7 us (3%)
  between operations  15.2 us (1%)
    all_gather x1, waiting for transfers between devices, body(): lax.all_gather(weights_two + weights_one, ('gx', 'gy', 'gz'))  830 us
    ppermute x9, starting transfers between devices, extended(): lax.ppermute(tail, axis, [(i, (i + 1) % count) for i in range(ends)])  34.2 us
    reduce_sum x1, other arithmetic, body(): jnp.sum(lax.all_gather(weights_two + weights_one, ('gx', 'gy', 'gz')), ax...  30.8 us
  transfers between devices with their start and end apart: 19, of which 3 were waited for; matrix products, arithmetic and copies ran while one was open for 3% of the time, Pallas kernels for 0%

profile of v1, /device:TPU:1, one launch (start us, length us, event | category | flops | bytes accessed | tf_op | source)
XLA Modules:
  0.0 1015.7 jit_solution(13061591113713065218)
XLA Ops:
  8.3 4.7 bitcast_dynamic-update-slice_fusion.5
  13.5 1.4 copy-done
  16.2 1.9 fusion.77
  18.1 2.0 fusion.13
  23.6 4.9 collective-permute-start.4
  31.1 4.3 collective-permute-start.2
  36.1 5.6 collective-permute-start.1
  43.1 4.4 fusion.78
  50.2 2.2 collective-permute-start
  55.1 2.0 fusion.72
  57.2 11.9 %fusion.37 = (bf16[4,8,64,128]{3,2,1,0:T(8,128)(2,1)S(1)}, f32[4,8,64,128]{3,2,1,0:T(8,128)S(1)}, f32[4,8,64,128]{3,2,1,0:T(8,128)}) fusion(bf16[4,8,1,128]{3,2,1,0:T(2,128)(2,1)S(1)} %broadcast_select_fusion.4, bf16[4,8,63,128]{3,2,1,0:T(8,128)(2,1)S(1)} %copy-done.19, f32[4,8,64,128]{3,2,1,0:T(8,128)S(1)} %get-tuple-element.13, ...), kind=kOutput, calls=%fused_computation.75 | output fusion | flops 4196479 | bytes 5775360 | tf_op jit(solution)/shard_map/sub | solution.py:116
  70.0 2.5 collective-permute-start.6
  72.5 3.2 collective-permute-start.7
  76.1 1.4 collective-permute-start.8
  77.6 4.0 collective-permute-start.9
  81.6 1.3 collective-permute-start.10
  82.9 4.0 collective-permute-start.11
  88.0 3.8 fusion.1
  91.8 5.5 fusion.79
  99.9 2.9 collective-permute-start.12
  104.0 3.4 collective-permute-start.13
  107.5 5.7 fusion.17
  113.5 1.3 collective-permute-start.14
  114.8 4.0 collective-permute-start.15
  118.8 1.3 collective-permute-start.16
  120.1 4.2 collective-permute-start.17
  125.3 3.8 fusion.4
  129.1 6.3 fusion.27
  135.5 8.0 fusion.80
  143.5 4.0 fusion.46
  147.5 829.7 %all-gather.3.cloned.1.call-done = f32[1536,128,128]{2,1,0:T(8,128)} async-done(((f32[6,128,128]{2,1,0:T(8,128)}), f32[1536,128,128]{2,1,0:T(8,128)}) %all-gather.3.cloned.1.call-update) | async-done | bytes 100663312 | tf_op jit(solution)/shard_map/all_gather | solution.py:191
  977.3 30.8 %reduce_sum.69 = f32[6,128,128]{2,1,0:T(8,128)S(1)} reduce(f32[256,6,128,128]{3,2,1,0:T(8,128)} %bitcast.75, f32[]{:T(128)} %constant.7.clone.1), dimensions={0}, to_apply=%region_6.7 | reduce | flops 25067520 | bytes 101056512 | tf_op jit(solution)/shard_map/reduce_sum | solution.py:191
  (154 shorter events, 24.2 us)
Async XLA Ops:
  7.2 970.1 %all-gather.3.cloned.1.call-start = ((), (), s32[]{:S(2)}) async-start(), calls=%async_computation | async-start | bytes 101056512 | tf_op jit(solution)/shard_map/all_gather | solution.py:191
  21.0 21.8 %copy-start.21 = (bf16[4,8,64,128]{3,2,1,0:T(8,128)(2,1)}, bf16[4,8,64,128]{3,2,1,0:T(8,128)(2,1)S(1)}, u32[]{:S(2)}) copy-start(bf16[4,8,64,128]{3,2,1,0:T(8,128)(2,1)S(1)} %get-tuple-element.23) | copy-start | bytes 1572868
  21.7 28.5 %collective-permute-start.5 = (bf16[4,8,1,128]{3,2,1,0:T(2,128)(2,1)}, bf16[4,8,1,128]{3,2,1,0:T(2,128)(2,1)}, u32[]{:S(2)}, u32[]{:S(2)}) collective-permute-start(bf16[4,8,1,128]{3,2,1,0:T(2,128)(2,1)} %slice.299), channel_id=1, source_target_pairs={{1,0},{3,2},{5,4},{7,6},{9,8},{11,10},{13,12},{15,14},{17,16},{19,... | collective-permute-start | bytes 24584 | tf_op jit(solution)/shard_map/ppermute | solution.py:19
  23.6 29.6 %collective-permute-start.4 = (bf16[4,8,1,128]{3,2,1,0:T(2,128)(2,1)}, bf16[4,8,1,128]{3,2,1,0:T(2,128)(2,1)S(1)}, u32[]{:S(2)}, u32[]{:S(2)}) collective-permute-start(bf16[4,8,1,128]{3,2,1,0:T(2,128)(2,1)} %slice.295), channel_id=1, source_target_pairs={{0,1},{2,3},{4,5},{6,7},{8,9},{10,11},{12,13},{14,15},{16,17},{18,... | collective-permute-start | bytes 24584 | tf_op jit(solution)/shard_map/ppermute | solution.py:17
  29.2 24.1 %collective-permute-start.3 = (bf16[4,1,64,128]{3,2,1,0:T(8,128)(2,1)}, bf16[4,1,64,128]{3,2,1,0:T(8,128)(2,1)}, u32[]{:S(2)}, u32[]{:S(2)}) collective-permute-start(bf16[4,1,64,128]{3,2,1,0:T(8,128)(2,1)} %slice.293), channel_id=1, source_target_pairs={{2,0},{4,2},{6,4},{3,1},{5,3},{7,5},{10,8},{12,10},{14,12},{11,9},... | collective-permute-start | bytes 196616 | tf_op jit(solution)/shard_map/ppermute | solution.py:19
  31.1 23.0 %collective-permute-start.2 = (bf16[4,1,64,128]{3,2,1,0:T(8,128)(2,1)}, bf16[4,1,64,128]{3,2,1,0:T(8,128)(2,1)S(1)}, u32[]{:S(2)}, u32[]{:S(2)}) collective-permute-start(bf16[4,1,64,128]{3,2,1,0:T(8,128)(2,1)} %slice.289), channel_id=1, source_target_pairs={{0,2},{2,4},{4,6},{1,3},{3,5},{5,7},{8,10},{10,12},{12,14},{9,11},... | collective-permute-start | bytes 196616 | tf_op jit(solution)/shard_map/ppermute | solution.py:17
  36.1 18.1 %collective-permute-start.1 = (bf16[1,8,64,128]{3,2,1,0:T(8,128)(2,1)}, bf16[1,8,64,128]{3,2,1,0:T(8,128)(2,1)}, u32[]{:S(2)}, u32[]{:S(2)}) collective-permute-start(bf16[1,8,64,128]{3,2,1,0:T(8,128)(2,1)} %get-tuple-element.20), channel_id=1, source_target_pairs={{8,0},{16,8},{24,16},{32,24},{40,32},{48,40},{56,48},{64,56},{72,6... | collective-permute-start | bytes 393224 | tf_op jit(solution)/shard_map/ppermute | solution.py:19
  50.2 4.9 collective-permute-start
  57.2 11.9 %copy-start.15 = (f32[4,8,64,128]{3,2,1,0:T(8,128)}, f32[4,8,64,128]{3,2,1,0:T(8,128)S(1)}, u32[]{:S(2)}) copy-start(f32[4,8,64,128]{3,2,1,0:T(8,128)S(1)} %get-tuple-element.13) | copy-start | bytes 3145732
  57.2 11.9 %copy-start.17 = (bf16[3,8,64,128]{3,2,1,0:T(8,128)(2,1)S(1)}, bf16[3,8,64,128]{3,2,1,0:T(8,128)(2,1)}, u32[]{:S(2)}) copy-start(bf16[3,8,64,128]{3,2,1,0:T(8,128)(2,1)} %get-tuple-element.21) | copy-start | bytes 1179652
  57.2 11.9 %copy-start.18 = (bf16[3,8,64,128]{3,2,1,0:T(8,128)(2,1)S(1)}, bf16[3,8,64,128]{3,2,1,0:T(8,128)(2,1)}, u32[]{:S(2)}) copy-start(bf16[3,8,64,128]{3,2,1,0:T(8,128)(2,1)} %get-tuple-element.22) | copy-start | bytes 1179652
  69.1 18.9 %slice-start = ((s8[6291456]{0:T(1024)(128)(4,1)}), s8[4194304]{0:T(1024)(128)(4,1)S(1)}, s32[]{:S(2)}) async-start(s8[6291456]{0:T(1024)(128)(4,1)} %bitcast.354), calls=%async_computation.1 | async-start | bytes 8388608
  70.0 12.9 %collective-permute-start.6 = (bf16[1,8,64,128]{3,2,1,0:T(8,128)(2,1)S(1)}, bf16[1,8,64,128]{3,2,1,0:T(8,128)(2,1)S(1)}, u32[]{:S(2)}, u32[]{:S(2)}) collective-permute-start(bf16[1,8,64,128]{3,2,1,0:T(8,128)(2,1)S(1)} %slice.301), channel_id=1, source_target_pairs={{8,0},{16,8},{24,16},{32,24},{40,32},{48,40},{56,48},{64,56},{72,6... | collective-permute-start | bytes 393224 | tf_op jit(solution)/shard_map/ppermute | solution.py:19
  72.5 14.4 %collective-permute-start.7 = (bf16[1,8,64,128]{3,2,1,0:T(8,128)(2,1)S(1)}, bf16[1,8,64,128]{3,2,1,0:T(8,128)(2,1)S(1)}, u32[]{:S(2)}, u32[]{:S(2)}) collective-permute-start(bf16[1,8,64,128]{3,2,1,0:T(8,128)(2,1)S(1)} %slice.302), channel_id=1, source_target_pairs={{0,8},{8,16},{16,24},{24,32},{32,40},{40,48},{48,56},{56,64},{64,7... | collective-permute-start | bytes 393224 | tf_op jit(solution)/shard_map/ppermute | solution.py:17
  75.7 53.4 %copy-start.24 = (f32[6,4,8,64]{3,2,1,0:T(8,128)}, f32[6,4,8,64]{3,2,1,0:T(8,128)S(1)}, u32[]{:S(2)}) copy-start(f32[6,4,8,64]{3,2,1,0:T(8,128)S(1)} %broadcast_divide_fusion) | copy-start | bytes 147460
  75.8 12.2 %slice-start.1 = ((s8[6291456]{0:T(1024)(128)(4,1)}), s8[2097152]{0:T(1024)(128)(4,1)S(1)}, s32[]{:S(2)}) async-start(s8[6291456]{0:T(1024)(128)(4,1)} %bitcast.354), calls=%async_computation.2 | async-start | bytes 4194304
  76.1 10.9 %collective-permute-start.8 = (bf16[4,1,64,128]{3,2,1,0:T(8,128)(2,1)S(1)}, bf16[4,1,64,128]{3,2,1,0:T(8,128)(2,1)S(1)}, u32[]{:S(2)}, u32[]{:S(2)}) collective-permute-start(bf16[4,1,64,128]{3,2,1,0:T(8,128)(2,1)S(1)} %slice.305), channel_id=1, source_target_pairs={{2,0},{4,2},{6,4},{3,1},{5,3},{7,5},{10,8},{12,10},{14,12},{11,9},... | collective-permute-start | bytes 196616 | tf_op jit(solution)/shard_map/ppermute | solution.py:19
  77.6 9.6 collective-permute-start.9
  81.6 5.6 collective-permute-start.10
  82.9 4.8 collective-permute-start.11
  99.9 13.3 %copy-start.20 = (bf16[4,8,64,128]{3,2,1,0:T(8,128)(2,1)}, bf16[4,8,64,128]{3,2,1,0:T(8,128)(2,1)S(1)}, u32[]{:S(2)}) copy-start(bf16[4,8,64,128]{3,2,1,0:T(8,128)(2,1)S(1)} %multiply_convert_fusion.5) | copy-start | bytes 1572868
  99.9 20.2 %collective-permute-start.12 = (bf16[1,8,64,128]{3,2,1,0:T(8,128)(2,1)S(1)}, bf16[1,8,64,128]{3,2,1,0:T(8,128)(2,1)S(1)}, u32[]{:S(2)}, u32[]{:S(2)}) collective-permute-start(bf16[1,8,64,128]{3,2,1,0:T(8,128)(2,1)S(1)} %slice.319), channel_id=1, source_target_pairs={{8,0},{16,8},{24,16},{32,24},{40,32},{48,40},{56,48},{64,56},{72,6... | collective-permute-start | bytes 393224 | tf_op jit(solution)/shard_map/ppermute | solution.py:19
  102.8 22.4 %slice-start.2 = ((s8[6291456]{0:T(1024)(128)(4,1)}), s8[2097152]{0:T(1024)(128)(4,1)S(1)}, s32[]{:S(2)}) async-start(s8[6291456]{0:T(1024)(128)(4,1)} %bitcast.356), calls=%async_computation.3 | async-start | bytes 4194304
  104.0 21.2 %slice-start.3 = ((s8[6291456]{0:T(1024)(128)(4,1)}), s8[4194304]{0:T(1024)(128)(4,1)S(1)}, s32[]{:S(2)}) async-start(s8[6291456]{0:T(1024)(128)(4,1)} %bitcast.356), calls=%async_computation.4 | async-start | bytes 8388608
  104.0 20.4 %collective-permute-start.13 = (bf16[1,8,64,128]{3,2,1,0:T(8,128)(2,1)S(1)}, bf16[1,8,64,128]{3,2,1,0:T(8,128)(2,1)S(1)}, u32[]{:S(2)}, u32[]{:S(2)}) collective-permute-start(bf16[1,8,64,128]{3,2,1,0:T(8,128)(2,1)S(1)} %slice.320), channel_id=1, source_target_pairs={{0,8},{8,16},{16,24},{24,32},{32,40},{40,48},{48,56},{56,64},{64,7... | collective-permute-start | bytes 393224 | tf_op jit(solution)/shard_map/ppermute | solution.py:17
  113.2 11.2 %slice-start.4 = ((bf16[4,8,64,128]{3,2,1,0:T(8,128)(2,1)}), bf16[3,8,64,128]{3,2,1,0:T(8,128)(2,1)S(1)}, s32[]{:S(2)}) async-start(bf16[4,8,64,128]{3,2,1,0:T(8,128)(2,1)} %copy-done.20), calls=%async_computation.5 | async-start | bytes 786432 | tf_op jit(solution)/shard_map/slice | solution.py:99
  113.5 11.0 %collective-permute-start.14 = (bf16[4,1,64,128]{3,2,1,0:T(8,128)(2,1)S(1)}, bf16[4,1,64,128]{3,2,1,0:T(8,128)(2,1)S(1)}, u32[]{:S(2)}, u32[]{:S(2)}) collective-permute-start(bf16[4,1,64,128]{3,2,1,0:T(8,128)(2,1)S(1)} %slice.323), channel_id=1, source_target_pairs={{2,0},{4,2},{6,4},{3,1},{5,3},{7,5},{10,8},{12,10},{14,12},{11,9},... | collective-permute-start | bytes 196616 | tf_op jit(solution)/shard_map/ppermute | solution.py:19
  114.8 9.8 collective-permute-start.15
  118.8 5.9 collective-permute-start.16
  120.1 4.8 collective-permute-start.17
  135.4 8.1 copy-start.2
  977.3 30.8 %copy-start.22 = (f32[6,128,128]{2,1,0:T(8,128)S(1)}, f32[6,128,128]{2,1,0:T(8,128)}, u32[]{:S(2)}) copy-start(f32[6,128,128]{2,1,0:T(8,128)} %param.6) | copy-start | bytes 1179652
  (18 other events, 92.6 us)
Sparse Core Ops, SparseCore 0:
  135.5 841.6 all-gather.2
